TPU v7x, 256 devices: a whole 4x4x8 slice. The times are simulated.
256 devices in a mesh: fsdp: 16 (over z_hi, x), tensor: 16 (over z_lo, y, core).
Axes of the slice: x: 4, y: 4, z: 8 (z_hi: 4, z_lo: 2; z = z_hi * 2 + z_lo), core: 2. Of those that a mesh axis runs over, the one named last changes fastest.
Arguments:
- tokens: bfloat16 [8192, 3072], P('fsdp'), may hold values from -6 to 6
- weights: bfloat16 [3072, 4, 4096], P('fsdp', None, 'tensor'), may hold values from -0.109375 to 0.109375
- direction: bfloat16 [3072, 4, 4096], P('fsdp', None, 'tensor'), may hold values from -0.109375 to 0.109375
- precision: float32 [3072], replicated, may hold values from 0.25 to 4
Outputs:
- ggn: float32 [3072, 4, 4096], P('fsdp', None, 'tensor')
All inputs are finite; a program needn't handle non-finite values.
Results may differ from a plain program's by a relative error of at most 0.015.
Values may be sent and summed in bfloat16 or wider, within the bound.
No kernel may reach another device: no remote copies, remote signals or barrier semaphores. Data moves between devices by JAX's collectives and lax.ppermute only.
A program may use at most 128 MiB of HBM per device.

v0:
```python
import jax
import jax.numpy as jnp
from jax import lax
from jax.sharding import PartitionSpec as P

HEAD = 128
PATCHES = 256


def layer_norm(rows):
    mean_row = jnp.mean(rows, -1, keepdims=True)
    centred = rows - mean_row
    spread = jnp.mean(centred * centred, -1, keepdims=True)
    return centred * lax.rsqrt(spread + 1e-06)


def attend(queries, key_rows, value_rows):
    query_norm = layer_norm(queries)
    key_norm = layer_norm(key_rows)
    score_scale = queries.shape[-1] ** (-0.5)
    scores = (
        jnp.einsum("bqhe,bkhe->bhqk", query_norm, key_norm, precision=lax.Precision.HIGHEST)
        * score_scale
    )
    exponent = jnp.exp(scores)
    attn_weights = exponent / jnp.sum(exponent, -1, keepdims=True)
    return jnp.einsum("bhqk,bkhe->bqhe", attn_weights, value_rows, precision=lax.Precision.HIGHEST)


def cross_rows(left, right):
    return lax.dot_general(
        left, right, (((1,), (1,)), ((), ())), preferred_element_type=jnp.float32
    )


def over_tokens(left, right):
    return lax.dot_general(
        left, right, (((0,), (0,)), ((), ())), preferred_element_type=jnp.float32
    )


def body(tokens, weights, direction, precision):
    model_width = tokens.shape[1]
    local_rows = tokens.shape[0]
    head_cols = weights.shape[2]
    normed = layer_norm(tokens.astype(jnp.float32)).astype(jnp.bfloat16)
    full_weights = lax.all_gather(weights, "fsdp", axis=0, tiled=True)
    full_direction = lax.all_gather(direction, "fsdp", axis=0, tiled=True)
    in_weights = full_weights[:, 0:3, :].reshape(model_width, 3 * head_cols)
    in_direction = full_direction[:, 0:3, :].reshape(model_width, 3 * head_cols)
    projected = jnp.dot(normed, in_weights, preferred_element_type=jnp.float32).astype(jnp.bfloat16)
    tangent_in = jnp.dot(normed, in_direction, preferred_element_type=jnp.float32).astype(
        jnp.bfloat16
    )

    def to_heads(block):
        return block.astype(jnp.float32).reshape(
            local_rows // PATCHES, PATCHES, 3, head_cols // HEAD, HEAD
        )

    primal = to_heads(projected)
    tangent_heads = to_heads(tangent_in)
    primal_args = (primal[:, :, 0], primal[:, :, 1], primal[:, :, 2])
    tangent_args = (tangent_heads[:, :, 0], tangent_heads[:, :, 1], tangent_heads[:, :, 2])
    mixed, mixed_dot = jax.jvp(attend, primal_args, tangent_args)
    mixed_rows = mixed.reshape(local_rows, head_cols).astype(jnp.bfloat16)
    tangent_out = mixed_dot.reshape(local_rows, head_cols).astype(jnp.bfloat16)
    out_weights = full_weights[:, 3, :]
    out_direction = full_direction[:, 3, :]
    partial_sum = cross_rows(tangent_out, out_weights) + cross_rows(mixed_rows, out_direction)
    output_dot = lax.psum(partial_sum.astype(jnp.bfloat16), "tensor").astype(jnp.float32)
    cotangent = (precision * output_dot).astype(jnp.bfloat16)
    share_rows = model_width // lax.axis_size("fsdp")
    back_rows = jnp.dot(cotangent, out_weights, preferred_element_type=jnp.float32)
    back_rows = back_rows.reshape(local_rows // PATCHES, PATCHES, head_cols // HEAD, HEAD)
    primal_out, pullback = jax.vjp(attend, *primal_args)
    gradients = pullback(back_rows)
    stacked = jnp.stack(gradients, axis=2).reshape(local_rows, 3 * head_cols).astype(jnp.bfloat16)
    return lax.psum_scatter(
        jnp.concatenate(
            [
                over_tokens(normed, stacked).reshape(
                    lax.axis_size("fsdp") * share_rows, 3, head_cols
                ),
                over_tokens(cotangent, mixed_rows)[:, None, :],
            ],
            axis=1,
        ).astype(jnp.bfloat16),
        "fsdp",
        scatter_dimension=0,
        tiled=True,
    ).astype(jnp.float32)


def solution(mesh):
    return jax.shard_map(
        body,
        mesh=mesh,
        in_specs=(P("fsdp", None), P("fsdp", None, "tensor"), P("fsdp", None, "tensor"), P()),
        out_specs=P("fsdp", None, "tensor"),
        check_vma=False,
    )
```

profile of v0, /device:TPU:1, one launch (start us, length us, event | category | flops | bytes accessed | tf_op | source)
XLA Modules:
  0.0 533.6 jit_solution(97903180383077813)
XLA Ops:
  6.5 0.7 all-gather.5.cloned.1.call-update
  7.3 0.7 all-gather.3.cloned.1.call-update
  8.1 2.4 convert_reduce_fusion
  10.4 1.0 fusion.2
  11.4 92.9 %all-gather.5.cloned.1.call-done = bf16[3072,4,256]{2,1,0:T(4,128)(2,1)} async-done(((bf16[192,4,256]{2,1,0:T(4,128)(2,1)}), bf16[3072,4,256]{2,1,0:T(4,128)(2,1)}) %all-gather.5.cloned.1.call-update) | async-done | bytes 6291472 | tf_op jit(solution)/shard_map/all_gather | solution.py:47
  104.3 10.1 %copy.106 = bf16[3072,3,256]{0,2,1:T(8,128)(2,1)} copy(bf16[3072,3,256]{2,1,0:T(4,128)(2,1)} %bitcast.153) | data formatting | bytes 9437184
  114.4 5.9 %convolution_convert_fusion.2 = bf16[512,768]{1,0:T(8,128)(2,1)} fusion(bf16[3072,768]{0,1:T(8,128)(2,1)} %bitcast.157, bf16[512,3072]{1,0:T(8,128)(2,1)S(1)} %copy-done.1, f32[512]{0:T(512)S(1)} %add_rsqrt_fusion, f32[512]{0:T(512)S(1)} %broadcast_multiply_fusion.4), kind=kOutput, calls=%fused_computation.16 | convolution fusion | flops 2422603776 | bytes 8654848 | tf_op jit(solution)/shard_map/dot_general | solution.py:51
  120.3 2.0 reshape.137
  122.3 1.0 copy.60
  123.6 78.6 %all-gather.3.cloned.1.call-done = bf16[3072,4,256]{2,1,0:T(4,128)(2,1)} async-done(((bf16[192,4,256]{2,1,0:T(4,128)(2,1)}), bf16[3072,4,256]{2,1,0:T(4,128)(2,1)}) %all-gather.3.cloned.1.call-update) | async-done | bytes 6291472 | tf_op jit(solution)/shard_map/all_gather | solution.py:48
  202.2 10.1 %copy.105 = bf16[3072,3,256]{0,2,1:T(8,128)(2,1)} copy(bf16[3072,3,256]{2,1,0:T(4,128)(2,1)} %bitcast.154) | data formatting | bytes 9437184
  212.3 5.9 %convolution_convert_fusion.3 = bf16[512,768]{1,0:T(8,128)(2,1)S(1)} fusion(bf16[3072,768]{0,1:T(8,128)(2,1)} %bitcast.158, bf16[512,3072]{1,0:T(8,128)(2,1)} %param.4, f32[512]{0:T(512)S(1)} %add_rsqrt_fusion, f32[512]{0:T(512)S(1)} %broadcast_multiply_fusion.4), kind=kOutput, calls=%fused_computation.17 | convolution fusion | flops 2422603776 | bytes 8654848 | tf_op jit(solution)/shard_map/dot_general | solution.py:52
  218.3 0.2 reshape.135
  218.4 2.1 copy.58
  220.5 1.3 reshape.139
  221.9 0.3 multiply_reduce_fusion.1
  222.3 1.2 fusion.65
  223.4 2.4 fusion.11
  225.8 2.3 fusion.42
  228.1 1.1 copy.74
  229.3 1.1 fusion.23
  230.5 1.3 fusion.66
  231.8 1.6 fusion.13
  233.6 6.2 %slice.48 = bf16[3072,1,256]{2,1,0:T(2,128)(2,1)S(1)} slice(bf16[3072,4,256]{2,1,0:T(4,128)(2,1)} %all-gather.5.cloned.1.call-done), slice={[0:3072], [3:4], [0:256]} | slice | bytes 3145728 | tf_op jit(solution)/shard_map/slice | solution.py:68
  239.9 1.0 fusion.6
  240.9 0.6 copy-done
  241.5 1.0 slice-done.1
  242.6 3.4 slice.49
  246.0 2.7 add_convert_fusion
  248.8 6.4 %copy.109 = bf16[3072,1,256]{0,2,1:T(8,128)(2,1)S(1)} copy(bf16[3072,1,256]{2,1,0:T(2,128)(2,1)} %copy-done) | data formatting | bytes 3145728 | tf_op jit(solution)/shard_map/dot_general | solution.py:74
  255.3 129.1 %all-reduce.2.cloned.1.call-done = bf16[512,3072]{1,0:T(8,128)(2,1)} async-done(((bf16[512,3072]{1,0:T(8,128)(2,1)}), bf16[512,3072]{1,0:T(8,128)(2,1)}) %all-reduce.2.cloned.1.call-update) | async-done | bytes 3145744 | tf_op jit(solution)/shard_map/psum | solution.py:71
  384.4 2.6 multiply_convert_fusion
  387.0 1.0 convolution_bitcast_fusion.2
  388.0 0.2 copy-done.5
  388.2 1.6 multiply_reduce_fusion
  389.8 1.3 fusion.12
  391.1 2.2 fusion.4
  393.3 1.0 multiply_reduce_fusion.4
  394.3 1.5 fusion.58
  396.0 0.3 fusion.36
  396.3 1.0 pad_maximum_fusion.1
  397.3 3.3 copy.83
  400.6 3.1 convert_element_type.64
  403.7 2.3 copy.84
  406.0 4.8 convolution_convert_fusion
  410.8 3.2 pad_maximum_fusion
  414.0 110.8 %reduce-scatter.2.cloned.1.call-done = bf16[192,4,256]{2,0,1:T(8,128)(2,1)} async-done(((bf16[3072,4,256]{2,0,1:T(8,128)(2,1)}), bf16[192,4,256]{2,0,1:T(8,128)(2,1)}) %reduce-scatter.2.cloned.1.call-update) | async-done | bytes 393232 | tf_op jit(solution)/shard_map/reduce_scatter | solution.py:79
  524.8 2.2 copy.86
  (46 shorter events, 1.0 us)
Async XLA Ops:
  6.5 3.9 copy-start.1
  6.5 97.8 %all-gather.5.cloned.1.call-start = ((), (), s32[]{:S(2)}) async-start(), calls=%async_computation.2 | async-start | bytes 6684672 | tf_op jit(solution)/shard_map/all_gather | solution.py:47
  7.3 194.9 %all-gather.3.cloned.1.call-start = ((), (), s32[]{:S(2)}) async-start(), calls=%async_computation.1 | async-start | bytes 6684672 | tf_op jit(solution)/shard_map/all_gather | solution.py:48
  8.0 376.4 %all-reduce.2.cloned.1.call-start = ((), (), s32[]{:S(2)}) async-start(), calls=%async_computation.3 | async-start | bytes 6291456 | tf_op jit(solution)/shard_map/psum | solution.py:71
  123.4 89.0 %copy-start.6 = (bf16[2,256,3,2,128]{1,4,3,0,2:T(8,128)(2,1)}, bf16[2,256,3,2,128]{1,4,3,0,2:T(8,128)(2,1)S(1)}, u32[]{:S(2)}) copy-start(bf16[2,256,3,2,128]{1,4,3,0,2:T(8,128)(2,1)S(1)} %copy.60) | copy-start | bytes 2359300
  223.4 4.7 copy-start.3
  229.3 1.2 copy-start.4
  229.3 2.5 copy-start.9
  233.6 8.0 %slice-start = ((s8[6291456]{0:T(1024)(128)(4,1)}), s8[4194304]{0:T(1024)(128)(4,1)S(1)}, s32[]{:S(2)}) async-start(s8[6291456]{0:T(1024)(128)(4,1)} %bitcast.155), calls=%async_computation.5 | async-start | bytes 8388608
  239.8 1.7 copy-start
  239.8 2.7 slice-start.1
  248.8 135.6 %copy-start.8 = (f32[3072]{0:T(1024)S(1)}, f32[3072]{0:T(1024)}, u32[]{:S(2)}) copy-start(f32[3072]{0:T(1024)} %param.7) | copy-start | bytes 36868
  248.8 276.1 %reduce-scatter.2.cloned.1.call-start = ((), (), s32[]{:S(2)}) async-start(), calls=%async_computation.4 | async-start | bytes 6684672 | tf_op jit(solution)/shard_map/reduce_scatter | solution.py:79
  386.9 1.2 copy-start.5
  396.3 9.7 %copy-start.2 = (bf16[512,3072]{1,0:T(8,128)(2,1)S(1)}, bf16[512,3072]{1,0:T(8,128)(2,1)}, u32[]{:S(2)}) copy-start(bf16[512,3072]{1,0:T(8,128)(2,1)} %param.4) | copy-start | bytes 9437188
  406.0 4.8 copy-start.7
Sparse Core Ops, SparseCore 0:
  9.8 94.4 all-gather.4
  106.7 95.4 all-gather.2
  248.9 135.4 all-reduce.1
  414.2 110.6 reduce-scatter.1
where the time goes:
time: 535 us; the launch traced here: 534 us
  waiting for transfers between devices  413 us (77%)
  local copies, waits for them, and re-layouts  55.8 us (10%)
  matrix products  38.9 us (7%)
  between operations  13.5 us (3%)
  other arithmetic  12.5 us (2%)
    psum x1, waiting for transfers between devices, body(): lax.psum(partial_sum.astype(jnp.bfloat16), 'tensor').astype(jnp.float32)  129 us
    reduce_scatter x1, waiting for transfers between devices, body(): lax.psum_scatter(jnp.concatenate([over_tokens(normed, stacked).reshape(la...  111 us
    all_gather x1, waiting for transfers between devices, body(): full_weights = lax.all_gather(weights, 'fsdp', axis=0, tiled=True)  92.9 us
    all_gather x1, waiting for transfers between devices, body(): full_direction = lax.all_gather(direction, 'fsdp', axis=0, tiled=True)  78.6 us
    unnamed x26, local copies, waits for them, and re-layouts  22.2 us
  transfers between devices with their start and end apart: 4, of which 4 were waited for; matrix products, arithmetic and copies ran while one was open for 5% of the time, Pallas kernels for 0%

commit v1 on v0

--- a/solution.py
+++ b/solution.py
@@ -40,6 +40,10 @@
 
 
 def body(tokens, weights, direction, precision):
+
+    def form_arrays(x_in, axis_id):
+        return lax.all_gather(x_in, axis_name=axis_id).sum(axis=0)
+
     model_width = tokens.shape[1]
     local_rows = tokens.shape[0]
     head_cols = weights.shape[2]
@@ -68,7 +72,7 @@
     out_weights = full_weights[:, 3, :]
     out_direction = full_direction[:, 3, :]
     partial_sum = cross_rows(tangent_out, out_weights) + cross_rows(mixed_rows, out_direction)
-    output_dot = lax.psum(partial_sum.astype(jnp.bfloat16), "tensor").astype(jnp.float32)
+    output_dot = form_arrays(partial_sum.astype(jnp.bfloat16), "tensor").astype(jnp.float32)
     cotangent = (precision * output_dot).astype(jnp.bfloat16)
     share_rows = model_width // lax.axis_size("fsdp")
     back_rows = jnp.dot(cotangent, out_weights, preferred_element_type=jnp.float32)

time: 535 us -> 661 us (1.24)
  waiting for transfers between devices: 413 us -> 535 us
  other arithmetic: 12.5 us -> 30.3 us
  local copies, waits for them, and re-layouts: 55.8 us -> 46.5 us
    all_gather x0 -> x1, waiting for transfers between devices: none -> 251 us  [form_arrays(): return lax.all_gather(x_in, axis_name=axis_id).sum(axis=0)]
    psum x1 -> x0, waiting for transfers between devices: 129 us -> none  [body(): lax.psum(partial_sum.astype(jnp.bfloat16), 'tensor').astype(jnp.float32)]
    reduce_sum x0 -> x1, other arithmetic: none -> 18.6 us  [form_arrays(): return lax.all_gather(x_in, axis_name=axis_id).sum(axis=0)]
    all_gather x1, waiting for transfers between devices: 78.6 us -> 92.4 us  [body(): full_direction = lax.all_gather(direction, 'fsdp', axis=0, tiled=True)]
    all_gather x1, waiting for transfers between devices: 92.9 us -> 80.3 us  [body(): full_weights = lax.all_gather(weights, 'fsdp', axis=0, tiled=True)]
    unnamed x26 -> x22, local copies, waits for them, and re-layouts: 22.2 us -> 22.5 us
  transfers between devices with their start and end apart: 4 -> 4, of which waited for: 4 -> 4; matrix products, arithmetic and copies ran while one was open for 5% -> 4% of each run, Pallas kernels for 0% -> 0%
where the time goes in v1:
time: 661 us; the launch traced here: 660 us
  waiting for transfers between devices  535 us (81%)
  local copies, waits for them, and re-layouts  46.5 us (7%)
  matrix products  35.2 us (5%)
  other arithmetic  30.3 us (5%)
  between operations  13.5 us (2%)
    all_gather x1, waiting for transfers between devices, form_arrays(): return lax.all_gather(x_in, axis_name=axis_id).sum(axis=0)  251 us
    reduce_scatter x1, waiting for transfers between devices, body(): lax.psum_scatter(jnp.concatenate([over_tokens(normed, stacked).reshape(la...  109 us
    all_gather x1, waiting for transfers between devices, body(): full_direction = lax.all_gather(direction, 'fsdp', axis=0, tiled=True)  92.4 us
    all_gather x1, waiting for transfers between devices, body(): full_weights = lax.all_gather(weights, 'fsdp', axis=0, tiled=True)  80.3 us
    unnamed x22, local copies, waits for them, and re-layouts  22.5 us
    reduce_sum x1, other arithmetic, form_arrays(): return lax.all_gather(x_in, axis_name=axis_id).sum(axis=0)  18.6 us
  transfers between devices with their start and end apart: 4, of which 4 were waited for; matrix products, arithmetic and copies ran while one was open for 4% of the time, Pallas kernels for 0%

profile of v1, /device:TPU:1, one launch (start us, length us, event | category | flops | bytes accessed | tf_op | source)
XLA Modules:
  0.0 660.2 jit_solution(18267985723765091871)
XLA Ops:
  6.5 0.7 all-gather.5.cloned.1.call-update
  7.3 0.7 all-gather.7.cloned.1.call-update
  8.1 2.5 convert_reduce_fusion
  10.6 0.3 copy-done.1
  10.9 1.0 fusion.2
  11.9 92.4 %all-gather.5.cloned.1.call-done = bf16[3072,4,256]{2,1,0:T(4,128)(2,1)} async-done(((bf16[192,4,256]{2,1,0:T(4,128)(2,1)}), bf16[3072,4,256]{2,1,0:T(4,128)(2,1)}) %all-gather.5.cloned.1.call-update) | async-done | bytes 6291472 | tf_op jit(solution)/shard_map/all_gather | solution.py:52
  104.3 10.1 %copy.105 = bf16[3072,3,256]{0,2,1:T(8,128)(2,1)} copy(bf16[3072,3,256]{2,1,0:T(4,128)(2,1)} %bitcast.155) | data formatting | bytes 9437184
  114.4 5.9 convolution_convert_fusion.3
  120.4 0.2 reshape.164
  120.6 1.0 copy.58
  121.8 80.3 %all-gather.7.cloned.1.call-done = bf16[3072,4,256]{2,1,0:T(4,128)(2,1)} async-done(((bf16[192,4,256]{2,1,0:T(4,128)(2,1)}), bf16[3072,4,256]{2,1,0:T(4,128)(2,1)}) %all-gather.7.cloned.1.call-update) | async-done | bytes 6291472 | tf_op jit(solution)/shard_map/all_gather | solution.py:51
  202.2 10.1 %copy.106 = bf16[3072,3,256]{0,2,1:T(8,128)(2,1)} copy(bf16[3072,3,256]{2,1,0:T(4,128)(2,1)} %bitcast.158) | data formatting | bytes 9437184
  212.3 5.9 convolution_convert_fusion.2
  218.2 0.2 reshape.166
  218.4 2.1 copy.60
  220.5 1.3 reshape.167
  221.9 0.3 multiply_reduce_fusion.1
  222.2 1.2 fusion.65
  223.4 1.7 fusion.42
  225.2 1.3 fusion.11
  226.5 1.1 fusion.23
  227.6 1.3 fusion.66
  228.9 0.7 fusion.13
  230.0 6.4 slice.48
  236.5 1.0 fusion.6
  237.5 0.6 copy-done
  238.1 1.1 slice-done.1
  239.2 3.4 slice.49
  242.6 2.7 add_convert_fusion
  245.3 6.2 copy.109
  251.6 251.2 %all-gather.9.cloned.1.call-done = bf16[8192,3072]{1,0:T(8,128)(2,1)} async-done(((bf16[512,3072]{1,0:T(8,128)(2,1)}), bf16[8192,3072]{1,0:T(8,128)(2,1)}) %all-gather.9.cloned.1.call-update) | async-done | bytes 50331664 | tf_op jit(solution)/shard_map/all_gather | solution.py:45
  502.8 18.6 %reduce_sum.183 = bf16[512,3072]{1,0:T(8,128)(2,1)} reduce(bf16[16,512,3072]{2,1,0:T(8,128)(2,1)} %bitcast.154, bf16[]{:T(256)} %constant.30.clone.1), dimensions={0}, to_apply=%region_12.0 | reduce | flops 23592960 | bytes 53477376 | tf_op jit(solution)/shard_map/reduce_sum | solution.py:45
  521.3 2.6 multiply_convert_fusion
  523.9 1.0 convolution_bitcast_fusion.2
  525.0 0.2 copy-done.3
  525.1 1.3 fusion.12
  526.5 1.7 multiply_reduce_fusion
  528.1 1.0 fusion.4
  529.2 1.0 multiply_reduce_fusion.4
  530.2 1.5 fusion.58
  531.8 0.3 fusion.36
  532.2 1.3 copy.83
  533.5 0.4 convert_element_type.85
  533.9 0.3 copy.84
  534.2 4.9 convolution_convert_fusion
  539.1 3.2 pad_maximum_fusion
  542.3 109.2 %reduce-scatter.2.cloned.1.call-done = bf16[192,4,256]{2,0,1:T(8,128)(2,1)} async-done(((bf16[3072,4,256]{2,0,1:T(8,128)(2,1)}), bf16[192,4,256]{2,0,1:T(8,128)(2,1)}) %reduce-scatter.2.cloned.1.call-update) | async-done | bytes 393232 | tf_op jit(solution)/shard_map/reduce_scatter | solution.py:83
  651.5 2.2 copy.86
  (43 shorter events, 1.2 us)
Async XLA Ops:
  6.5 97.8 %all-gather.5.cloned.1.call-start = ((), (), s32[]{:S(2)}) async-start(), calls=%async_computation.1 | async-start | bytes 6684672 | tf_op jit(solution)/shard_map/all_gather | solution.py:52
  7.3 194.9 %all-gather.7.cloned.1.call-start = ((), (), s32[]{:S(2)}) async-start(), calls=%async_computation.2 | async-start | bytes 6684672 | tf_op jit(solution)/shard_map/all_gather | solution.py:51
  8.0 494.8 %all-gather.9.cloned.1.call-start = ((), (), s32[]{:S(2)}) async-start(), calls=%async_computation.4 | async-start | bytes 53477376 | tf_op jit(solution)/shard_map/all_gather | solution.py:45
  8.1 2.8 copy-start.1
  121.6 90.7 %copy-start.5 = (bf16[2,256,3,2,128]{1,4,3,0,2:T(8,128)(2,1)}, bf16[2,256,3,2,128]{1,4,3,0,2:T(8,128)(2,1)S(1)}, u32[]{:S(2)}) copy-start(bf16[2,256,3,2,128]{1,4,3,0,2:T(8,128)(2,1)S(1)} %copy.58) | copy-start | bytes 2359300
  222.2 3.0 copy-start.4
  223.4 5.5 copy-start.2
  228.9 1.0 copy-start.6
  230.0 8.1 %slice-start = ((s8[6291456]{0:T(1024)(128)(4,1)}), s8[4194304]{0:T(1024)(128)(4,1)S(1)}, s32[]{:S(2)}) async-start(s8[6291456]{0:T(1024)(128)(4,1)} %bitcast.156), calls=%async_computation.5 | async-start | bytes 8388608
  236.4 1.6 copy-start
  236.4 2.7 slice-start.1
  245.3 406.2 %reduce-scatter.2.cloned.1.call-start = ((), (), s32[]{:S(2)}) async-start(), calls=%async_computation.3 | async-start | bytes 6684672 | tf_op jit(solution)/shard_map/reduce_scatter | solution.py:83
  502.8 18.6 %copy-start.7 = (f32[3072]{0:T(1024)S(1)}, f32[3072]{0:T(1024)}, u32[]{:S(2)}) copy-start(f32[3072]{0:T(1024)} %param.7) | copy-start | bytes 36868
  523.9 1.2 copy-start.3
Sparse Core Ops, SparseCore 0:
  9.8 94.4 all-gather.4
  106.7 95.3 all-gather.6
  245.4 257.3 all-gather.8
  542.4 109.0 reduce-scatter.1
